TPU v7x, 32 devices: a whole 2x2x4 slice. The times are simulated.
32 devices in a mesh: src: 4 (over x, core), ep: 8 (over z, y).
Axes of the slice: x: 2, y: 2, z: 4, core: 2. Of those that a mesh axis runs over, the one named last changes fastest.
Arguments:
- log_conductivity: float32 [8, 16, 32, 128], P('ep'), may hold values from -3 to 3
- forward_field: float32 [8, 4, 16, 32, 128], P('ep', 'src'), may hold values from -6 to 6
- adjoint_field: float32 [8, 4, 16, 32, 128], P('ep', 'src'), may hold values from -6 to 6
- source_cells: int32 [4, 2], P('src'), may hold values from 0 to 65535
- receiver_cells: int32 [128], replicated, may hold values from 0 to 65535
- observed: float32 [8, 4, 128], P('ep', 'src'), may hold values from -6 to 6
- split_term: float32 [6, 65536], P(None, ('src', 'ep')), may hold values from -1.2 to 1.2
- dual_term: float32 [6, 65536], P(None, ('src', 'ep')), may hold values from -1.2 to 1.2
Outputs:
- model_out: float32 [8, 16, 32, 128], P('ep')
- split_out: float32 [6, 65536], P(None, ('src', 'ep'))
- dual_out: float32 [6, 65536], P(None, ('src', 'ep'))
Inputs may be any that keep to these rules, and one draw needn't show every extreme that they name: `source_cells`: source and receiver cells may repeat; a source's two electrodes may coincide.
All inputs are finite; a program needn't handle non-finite values.
Results may differ from a plain program's by a relative error of at most 0.0003.
Values sent between devices are 32-bit elements; how exact they have to be, the bound alone decides.
No kernel may reach another device: no remote copies, remote signals or barrier semaphores. Data moves between devices by JAX's collectives and lax.ppermute only.
A program may use at most 128 MiB of HBM per device.

v0:
```python
import jax
import jax.numpy as jnp
from jax import lax
from jax.sharding import PartitionSpec as P

SWEEPS = 4
MASS_TERM = 0.5
RELAXATION = 0.8
CURRENT = 4.0
DATA_WEIGHT = 8.0
STEP_SIZE = 0.5
PENALTY = 64.0
THRESHOLD = 0.1


def pad_side(values, dim_index, at_low):
    widths = [(0, 0)] * values.ndim
    widths[dim_index] = (0, 1) if at_low else (1, 0)
    return jnp.pad(values, widths)


def conductances(conductivity):
    face_weights = []
    diagonal = MASS_TERM * conductivity
    ndims = conductivity.ndim
    for dim_index in range(ndims - 3, ndims):
        length = conductivity.shape[dim_index]
        lower_cells = lax.slice_in_dim(conductivity, 0, length - 1, axis=dim_index)
        upper_cells = lax.slice_in_dim(conductivity, 1, length, axis=dim_index)
        face_weight = 0.5 * (lower_cells + upper_cells)
        face_weights.append(face_weight)
        diagonal = (
            diagonal
            + pad_side(face_weight, dim_index, True)
            + pad_side(face_weight, dim_index, False)
        )
    return (face_weights, diagonal)


def operate(iterate, conductivity, face_weights):
    result = MASS_TERM * conductivity * iterate
    ndims = iterate.ndim
    for position, dim_index in enumerate(range(ndims - 3, ndims)):
        length = iterate.shape[dim_index]
        face_flux = face_weights[position] * (
            lax.slice_in_dim(iterate, 1, length, axis=dim_index)
            - lax.slice_in_dim(iterate, 0, length - 1, axis=dim_index)
        )
        result = (
            result - pad_side(face_flux, dim_index, True) + pad_side(face_flux, dim_index, False)
        )
    return result


def relax(iterate, right_side, conductivity, face_weights, diagonal):
    for sweep_index in range(SWEEPS):
        iterate = (
            iterate
            + RELAXATION * (right_side - operate(iterate, conductivity, face_weights)) / diagonal
        )
    return iterate


def source_field(source_cells, cell_count):
    source_count = source_cells.shape[0]
    row_index = jnp.arange(source_count, dtype=jnp.int32)[:, None] * jnp.ones((1, 2), jnp.int32)
    polarity = jnp.broadcast_to(jnp.array([CURRENT, -CURRENT], jnp.float32), (source_count, 2))
    return (
        jnp.zeros((source_count, cell_count), jnp.float32).at[row_index, source_cells].add(polarity)
    )


def sweep_epoch(model_log, forward, adjoint, sources, receiver_cells, observed):
    grid_shape = forward.shape
    conductivity = jnp.exp(model_log)[None]
    face_weights, diagonal = conductances(conductivity)
    forward = relax(forward, sources.reshape(grid_shape), conductivity, face_weights, diagonal)
    flat_field = forward.reshape(grid_shape[0], -1)
    misfit = flat_field[:, receiver_cells] - observed
    adjoint_source = (
        jnp.zeros_like(flat_field)
        .at[:, receiver_cells]
        .add(DATA_WEIGHT * misfit)
        .reshape(grid_shape)
    )
    adjoint = relax(adjoint, adjoint_source, conductivity, face_weights, diagonal)
    gradient = conductivity[0] * jnp.sum(forward * adjoint, axis=0)
    return (forward, adjoint, gradient)


def temporal_factor(epochs):
    second = (
        jnp.eye(epochs - 2, epochs, dtype=jnp.float32)
        - 2.0 * jnp.eye(epochs - 2, epochs, k=1, dtype=jnp.float32)
        + jnp.eye(epochs - 2, epochs, k=2, dtype=jnp.float32)
    )
    matrix = jnp.eye(epochs, dtype=jnp.float32) + PENALTY * jnp.dot(
        second.T, second, precision=lax.Precision.HIGHEST
    )
    return jnp.linalg.cholesky(matrix)


def difference(values):
    return values[:-2] - 2.0 * values[1:-1] + values[2:]


def difference_adjoint(values):
    widths_low = [(0, 2), (0, 0)]
    widths_mid = [(1, 1), (0, 0)]
    widths_high = [(2, 0), (0, 0)]
    return (
        jnp.pad(values, widths_low)
        - 2.0 * jnp.pad(values, widths_mid)
        + jnp.pad(values, widths_high)
    )


def splitting_update(local_rhs, split_term, dual_term, factor):
    right_side = local_rhs + PENALTY * difference_adjoint(split_term - dual_term)
    updated = jax.scipy.linalg.cho_solve((factor, True), right_side)
    shifted = difference(updated) + dual_term
    split_term = shifted - jnp.clip(shifted, -THRESHOLD, THRESHOLD)
    dual_term = shifted - split_term
    return (updated, split_term, dual_term)


def on_device(
    log_conductivity,
    forward_field,
    adjoint_field,
    source_cells,
    receiver_cells,
    observed,
    split_term,
    dual_term,
):
    slab_epochs, size_x, size_y, size_z = log_conductivity.shape
    cell_count = size_x * size_y * size_z
    share_cells = cell_count // lax.axis_size("src")
    offset = lax.axis_index("src") * share_cells
    total_epochs = slab_epochs * lax.axis_size("ep")
    sources = source_field(source_cells, cell_count)
    factor = temporal_factor(total_epochs)
    sweeper = jax.vmap(sweep_epoch, in_axes=(0, 0, 0, None, None, 0))
    model_log = log_conductivity
    forward = forward_field
    adjoint = adjoint_field
    forward, adjoint, partial_terms = sweeper(
        model_log, forward, adjoint, sources, receiver_cells, observed
    )
    partial_terms = partial_terms.reshape(slab_epochs, cell_count)
    summed = lax.psum(partial_terms, "src")
    gradient_share = lax.dynamic_slice_in_dim(summed, offset, share_cells, 1)
    model_share = lax.dynamic_slice_in_dim(
        model_log.reshape(slab_epochs, cell_count), offset, share_cells, 1
    )
    local_rhs = model_share - STEP_SIZE * gradient_share
    time_rhs = lax.all_to_all(local_rhs, "ep", split_axis=1, concat_axis=0, tiled=True)
    updated, split_term, dual_term = splitting_update(time_rhs, split_term, dual_term, factor)
    slab_share = lax.all_to_all(updated, "ep", split_axis=0, concat_axis=1, tiled=True)
    model_log = lax.all_gather(slab_share, "src", axis=1, tiled=True).reshape(
        slab_epochs, size_x, size_y, size_z
    )
    return (model_log, split_term, dual_term)


def solution(mesh):
    return jax.shard_map(
        on_device,
        mesh=mesh,
        in_specs=(
            P("ep", None, None, None),
            P("ep", "src", None, None, None),
            P("ep", "src", None, None, None),
            P("src", None),
            P(),
            P("ep", "src", None),
            P(None, ("src", "ep")),
            P(None, ("src", "ep")),
        ),
        out_specs=(P("ep", None, None, None), P(None, ("src", "ep")), P(None, ("src", "ep"))),
        check_vma=False,
    )
```

profile of v0, /device:TPU:0, one launch (start us, length us, event | category | flops | bytes accessed | tf_op | source)
XLA Modules:
  0.0 93.7 jit_solution(12895999680581403792)
XLA Ops:
  7.2 1.0 %exponential_bitcast_fusion = f32[1,1,16,32,128]{4,3,2,1,0:T(8,128)S(1)} fusion(f32[1,16,32,128]{3,2,1,0:T(8,128)} %param.9), kind=kLoop, calls=%fused_computation.45 | loop fusion | bytes 524288 | tf_op jit(solution)/shard_map/vmap()/broadcast_in_dim | solution.py:75
  8.3 0.2 subtract_multiply_fusion
  8.6 0.9 copy-done.2
  9.7 0.7 subtract_multiply_fusion.5
  10.8 0.8 scatter_custom_fusion
  11.6 1.4 %divide_add_fusion.6 = (f32[1,1,16,32,128]{4,3,2,1,0:T(8,128)S(1)}, f32[1,1,16,32,128]{4,3,2,1,0:T(8,128)S(1)}) fusion(f32[1,1,16,32,128]{4,3,2,1,0:T(8,128)S(1)} %copy-done.2, f32[1,1,16,32,128]{4,3,2,1,0:T(8,128)S(1)} %bitcast.67, f32[1,1,16,32,127]{4,3,2,1,0:T(8,128)S(1)} %subtract_multiply_fusion.2, ...), kind=kLoop, calls=%fused_computation.41 | loop fusion | flops 1179648 | bytes 2830336 | tf_op jit(solution)/shard_map/vmap()/add | solution.py:58
  13.3 0.3 divide_add_fusion.5
  13.8 0.3 divide_add_fusion.4
  14.3 0.5 copy-done.6
  14.8 0.2 divide_add_fusion.3
  15.1 1.1 %gather_fusion = f32[128]{0:T(128)S(1)} fusion(f32[65536]{0:T(1024)S(1)} %bitcast.71, s32[1024]{0:T(1024)S(1)} %pad_clamp_fusion), kind=kCustom, calls=%fused_computation | custom fusion | bytes 1536 | tf_op jit(solution)/shard_map/vmap()/gather | solution.py:79
  16.3 1.3 %scatter_custom_fusion.1 = f32[65536]{0:T(1024)S(1)} fusion(s32[128]{0:T(128)S(1)} %compare_select_fusion, f32[128]{0:T(128)S(1)} %fusion.55, f32[]{:T(128)} %constant.82.clone.1), kind=kCustom, calls=%fused_computation.62 | custom fusion | flops 128 | bytes 262148 | tf_op jit(solution)/shard_map/vmap()/scatter-add | solution.py:83
  17.6 0.3 divide_add_fusion.2
  18.1 0.3 divide_add_fusion.1
  18.6 0.3 divide_add_fusion
  19.1 1.0 %bitcast_multiply_fusion = f32[1,16,32,128]{3,2,1,0:T(8,128)} fusion(f32[1,1,16,32,128]{4,3,2,1,0:T(8,128)S(1)} %divide_add_fusion.3, f32[1,1,16,32,128]{4,3,2,1,0:T(8,128)S(1)} %divide_add_fusion, f32[1,1,16,32,128]{4,3,2,1,0:T(8,128)S(1)} %get-tuple-element.12, f32[1,1,16,32,128]{4,3,2,1,0:T(8,128)S(1)} %bitcast.66, f32[1,1,16,32,127]{4,3,2,1,0:T(8,128)S(1)} %fusion, ...), kind=kLoop, calls=%fused_computation.32 | loop fusion | flops 917504 | bytes 2332672 | tf_op jit(solution)/shard_map/vmap()/mul | solution.py:87
  20.1 0.3 convert_add_fusion
  20.5 0.7 cholesky.17
  21.4 0.6 compare_reduce_fusion
  22.0 32.9 %all-reduce.60.cloned.1.call-done = f32[1,65536]{1,0:T(1,128)} async-done(((f32[1,65536]{1,0:T(1,128)}), f32[1,65536]{1,0:T(1,128)}) %all-reduce.60.cloned.1.call-update) | async-done | bytes 262160 | tf_op jit(solution)/shard_map/psum | solution.py:152
  54.9 1.6 %multiply_subtract_fusion = f32[1,16384]{1,0:T(1,128)} fusion(f32[1,65536]{1,0:T(1,128)} %all-reduce.60.cloned.1.call-done, s32[]{:T(128)S(6)} %select_n.16, f32[1,65536]{1,0:T(1,128)S(1)} %bitcast.62), kind=kLoop, calls=%fused_computation.81 | loop fusion | flops 32768 | bytes 196612 | tf_op jit(solution)/shard_map/sub | solution.py:157
  56.5 5.6 %all-to-all-start = ((f32[1,8,2048]{2,0,1:T(1,128)}), f32[1,8,2048]{2,0,1:T(1,128)S(1)}, u32[]{:S(2)}, u32[]{:S(2)}) async-start(f32[1,8,2048]{2,0,1:T(1,128)} %bitcast.14), calls=%async_computation | async-start | bytes 131072 | tf_op jit(solution)/shard_map/all_to_all | solution.py:158
  62.1 0.6 select_select_fusion
  62.9 0.6 custom-call.10
  63.5 5.5 %all-to-all-done = f32[1,8,2048]{2,0,1:T(1,128)S(1)} async-done(((f32[1,8,2048]{2,0,1:T(1,128)}), f32[1,8,2048]{2,0,1:T(1,128)S(1)}, u32[]{:S(2)}, u32[]{:S(2)}) %all-to-all-start) | async-done | bytes 65568 | tf_op jit(solution)/shard_map/all_to_all | solution.py:158
  69.0 0.3 fusion.27
  69.5 0.7 copy.33
  70.2 3.4 %all-to-all-start.1 = ((f32[8,1,2048]{2,1,0:T(1,128)}), f32[8,1,2048]{2,1,0:T(1,128)S(1)}, u32[]{:S(2)}, u32[]{:S(2)}) async-start(f32[8,1,2048]{2,1,0:T(1,128)} %copy.33), calls=%async_computation.1 | async-start | bytes 131072 | tf_op jit(solution)/shard_map/all_to_all | solution.py:160
  73.6 0.7 fusion.61
  74.2 6.2 %all-to-all-done.1 = f32[8,1,2048]{2,1,0:T(1,128)S(1)} async-done(((f32[8,1,2048]{2,1,0:T(1,128)}), f32[8,1,2048]{2,1,0:T(1,128)S(1)}, u32[]{:S(2)}, u32[]{:S(2)}) %all-to-all-start.1) | async-done | bytes 65568 | tf_op jit(solution)/shard_map/all_to_all | solution.py:160
  80.4 5.8 %all_gather.3 = f32[1,65536]{1,0:T(1,128)S(1)} all-gather(f32[1,16384]{1,0:T(1,128)S(1)} %bitcast.75), channel_id=1, replica_groups=mesh['src'=4,'ep'=8] {'src'}, dimensions={1}, use_global_device_ids=true | all-gather | bytes 327680 | tf_op jit(solution)/shard_map/all_gather | solution.py:161
  86.2 0.7 copy.43
  (53 shorter events, 2.7 us)
Async XLA Ops:
  7.2 1.1 %copy-start.1 = (f32[1,1,16,32,128]{4,3,2,1,0:T(8,128)S(1)}, f32[1,1,16,32,128]{4,3,2,1,0:T(8,128)}, u32[]{:S(2)}) copy-start(f32[1,1,16,32,128]{4,3,2,1,0:T(8,128)} %param.11) | copy-start | bytes 786436
  7.2 47.8 %all-reduce.60.cloned.1.call-start = ((), (), s32[]{:S(2)}) async-start(), calls=%async_computation.2 | async-start | bytes 524288 | tf_op jit(solution)/shard_map/psum | solution.py:152
  8.6 1.0 %copy-start.2 = (f32[1,1,16,32,128]{4,3,2,1,0:T(8,128)S(1)}, f32[1,1,16,32,128]{4,3,2,1,0:T(8,128)}, u32[]{:S(2)}) copy-start(f32[1,1,16,32,128]{4,3,2,1,0:T(8,128)} %param.10) | copy-start | bytes 786436
  9.7 0.7 copy-start.5
  10.4 1.2 %copy-start = (f32[1,16,32,128]{3,2,1,0:T(8,128)S(1)}, f32[1,16,32,128]{3,2,1,0:T(8,128)}, u32[]{:S(2)}) copy-start(f32[1,16,32,128]{3,2,1,0:T(8,128)} %param.9) | copy-start | bytes 786436
  14.2 0.7 copy-start.6
  15.1 1.2 %copy-start.7 = (f32[1,1,128]{2,1,0:T(1,128)S(1)}, f32[1,1,128]{2,1,0:T(1,128)}, u32[]{:S(2)}) copy-start(f32[1,1,128]{2,1,0:T(1,128)} %param.14) | copy-start | bytes 1540
  56.5 7.0 %copy-start.3 = (f32[6,2048]{1,0:T(8,128)S(1)}, f32[6,2048]{1,0:T(8,128)}, u32[]{:S(2)}) copy-start(f32[6,2048]{1,0:T(8,128)} %param.16) | copy-start | bytes 147460
  56.5 7.0 %copy-start.4 = (f32[6,2048]{1,0:T(8,128)S(1)}, f32[6,2048]{1,0:T(8,128)}, u32[]{:S(2)}) copy-start(f32[6,2048]{1,0:T(8,128)} %param.15) | copy-start | bytes 147460
  56.5 12.6 %all-to-all-start = ((f32[1,8,2048]{2,0,1:T(1,128)}), f32[1,8,2048]{2,0,1:T(1,128)S(1)}, u32[]{:S(2)}, u32[]{:S(2)}) async-start(f32[1,8,2048]{2,0,1:T(1,128)} %bitcast.14), calls=%async_computation | async-start | bytes 131072 | tf_op jit(solution)/shard_map/all_to_all | solution.py:158
  70.2 10.2 %all-to-all-start.1 = ((f32[8,1,2048]{2,1,0:T(1,128)}), f32[8,1,2048]{2,1,0:T(1,128)S(1)}, u32[]{:S(2)}, u32[]{:S(2)}) async-start(f32[8,1,2048]{2,1,0:T(1,128)} %copy.33), calls=%async_computation.1 | async-start | bytes 131072 | tf_op jit(solution)/shard_map/all_to_all | solution.py:160
Sparse Core Ops, SparseCore 0:
  20.2 34.6 all-reduce.59
where the time goes:
time: 94.2 us; the launch traced here: 93.7 us
  waiting for transfers between devices  44.6 us (47%)
  between operations  14.4 us (15%)
  other arithmetic  13.8 us (15%)
  starting transfers between devices  9.04 us (10%)
  blocking collectives  5.77 us (6%)
  local copies, waits for them, and re-layouts  5.39 us (6%)
    psum x1, waiting for transfers between devices, on_device(): summed = lax.psum(partial_terms, 'src')  32.9 us
    all_to_all x1, waiting for transfers between devices, on_device(): lax.all_to_all(updated, 'ep', split_axis=0, concat_axis=1, tiled=True)  6.16 us
    all_gather x1, blocking collectives, on_device(): lax.all_gather(slab_share, 'src', axis=1, tiled=True)  5.77 us
    all_to_all x1, starting transfers between devices, on_device(): lax.all_to_all(local_rhs, 'ep', split_axis=1, concat_axis=0, tiled=True)  5.65 us
    all_to_all x1, waiting for transfers between devices, on_device(): lax.all_to_all(local_rhs, 'ep', split_axis=1, concat_axis=0, tiled=True)  5.53 us
    all_to_all x1, starting transfers between devices, on_device(): lax.all_to_all(updated, 'ep', split_axis=0, concat_axis=1, tiled=True)  3.35 us
    add x7, other arithmetic, relax(): iterate + RELAXATION * (right_side - operate(iterate, conductivity, face_...  2.93 us
    mul x24, other arithmetic, operate(): face_weights[position]  2.55 us
  transfers between devices with their start and end apart: 3, of which 3 were waited for; matrix products, arithmetic and copies ran while one was open for 4% of the time, Pallas kernels for 0%

commit v1 on v0

--- a/solution.py
+++ b/solution.py
@@ -149,7 +149,8 @@
         model_log, forward, adjoint, sources, receiver_cells, observed
     )
     partial_terms = partial_terms.reshape(slab_epochs, cell_count)
-    summed = lax.psum(partial_terms, "src")
+    pieces = lax.all_gather(partial_terms, "src", axis=0, tiled=False)
+    summed = pieces.sum(axis=0)
     gradient_share = lax.dynamic_slice_in_dim(summed, offset, share_cells, 1)
     model_share = lax.dynamic_slice_in_dim(
         model_log.reshape(slab_epochs, cell_count), offset, share_cells, 1

time: 94.2 us -> 80.3 us (0.85)
  waiting for transfers between devices: 44.6 us -> 29.4 us
  other arithmetic: 13.8 us -> 15.2 us
    psum x1 -> x0, waiting for transfers between devices: 32.9 us -> none  [on_device(): summed = lax.psum(partial_terms, 'src')]
    all_gather x0 -> x1, waiting for transfers between devices: none -> 17.7 us  [on_device(): pieces = lax.all_gather(partial_terms, 'src', axis=0, tiled=False)]
    reduce_sum x0 -> x1, other arithmetic: none -> 2.19 us  [on_device(): summed = pieces.sum(axis=0)]
  transfers between devices with their start and end apart: 3 -> 3, of which waited for: 3 -> 3; matrix products, arithmetic and copies ran while one was open for 4% -> 5% of each run, Pallas kernels for 0% -> 0%
where the time goes in v1:
time: 80.3 us; the launch traced here: 79.9 us
  waiting for transfers between devices  29.4 us (37%)
  other arithmetic  15.2 us (19%)
  between operations  14.4 us (18%)
  starting transfers between devices  9.04 us (11%)
  blocking collectives  5.77 us (7%)
  local copies, waits for them, and re-layouts  5.39 us (7%)
    all_gather x1, waiting for transfers between devices, on_device(): pieces = lax.all_gather(partial_terms, 'src', axis=0, tiled=False)  17.7 us
    all_to_all x1, waiting for transfers between devices, on_device(): lax.all_to_all(updated, 'ep', split_axis=0, concat_axis=1, tiled=True)  6.16 us
    all_gather x1, blocking collectives, on_device(): lax.all_gather(slab_share, 'src', axis=1, tiled=True)  5.77 us
    all_to_all x1, starting transfers between devices, on_device(): lax.all_to_all(local_rhs, 'ep', split_axis=1, concat_axis=0, tiled=True)  5.65 us
    all_to_all x1, waiting for transfers between devices, on_device(): lax.all_to_all(local_rhs, 'ep', split_axis=1, concat_axis=0, tiled=True)  5.53 us
    all_to_all x1, starting transfers between devices, on_device(): lax.all_to_all(updated, 'ep', split_axis=0, concat_axis=1, tiled=True)  3.35 us
    add x7, other arithmetic, relax(): iterate + RELAXATION * (right_side - operate(iterate, conductivity, face_...  2.93 us
    mul x24, other arithmetic, operate(): face_weights[position]  2.55 us
  transfers between devices with their start and end apart: 3, of which 3 were waited for; matrix products, arithmetic and copies ran while one was open for 5% of the time, Pallas kernels for 0%

profile of v1, /device:TPU:0, one launch (start us, length us, event | category | flops | bytes accessed | tf_op | source)
XLA Modules:
  0.0 79.9 jit_solution(9862936214051846149)
XLA Ops:
  7.2 1.0 %exponential_bitcast_fusion = f32[1,1,16,32,128]{4,3,2,1,0:T(8,128)S(1)} fusion(f32[1,16,32,128]{3,2,1,0:T(8,128)} %param.9), kind=kLoop, calls=%fused_computation.45 | loop fusion | bytes 524288 | tf_op jit(solution)/shard_map/vmap()/broadcast_in_dim | solution.py:75
  8.6 0.9 %copy-done.2 = f32[1,1,16,32,128]{4,3,2,1,0:T(8,128)S(1)} copy-done((f32[1,1,16,32,128]{4,3,2,1,0:T(8,128)S(1)}, f32[1,1,16,32,128]{4,3,2,1,0:T(8,128)}, u32[]{:S(2)}) %copy-start.2) | copy-done | bytes 262168
  9.7 0.7 subtract_multiply_fusion.5
  10.8 0.8 %scatter_custom_fusion = f32[65536]{0:T(1024)S(1)} fusion(s32[2]{0:T(128)S(1)} %fusion.52, f32[2]{0:T(128)} %constant.221, f32[]{:T(128)} %constant.82.clone.1), kind=kCustom, calls=%fused_computation.64 | custom fusion | flops 2 | bytes 262656 | tf_op jit(solution)/shard_map/scatter-add | solution.py:69
  11.6 1.4 %divide_add_fusion.6 = (f32[1,1,16,32,128]{4,3,2,1,0:T(8,128)S(1)}, f32[1,1,16,32,128]{4,3,2,1,0:T(8,128)S(1)}) fusion(f32[1,1,16,32,128]{4,3,2,1,0:T(8,128)S(1)} %copy-done.2, f32[1,1,16,32,128]{4,3,2,1,0:T(8,128)S(1)} %bitcast.68, f32[1,1,16,32,127]{4,3,2,1,0:T(8,128)S(1)} %subtract_multiply_fusion.2, ...), kind=kLoop, calls=%fused_computation.41 | loop fusion | flops 1179648 | bytes 2830336 | tf_op jit(solution)/shard_map/vmap()/add | solution.py:58
  13.3 0.3 divide_add_fusion.5
  13.8 0.3 divide_add_fusion.4
  14.3 0.5 copy-done.6
  14.8 0.2 divide_add_fusion.3
  15.1 1.1 %gather_fusion = f32[128]{0:T(128)S(1)} fusion(f32[65536]{0:T(1024)S(1)} %bitcast.72, s32[1024]{0:T(1024)S(1)} %pad_clamp_fusion), kind=kCustom, calls=%fused_computation | custom fusion | bytes 1536 | tf_op jit(solution)/shard_map/vmap()/gather | solution.py:79
  16.3 1.3 %scatter_custom_fusion.1 = f32[65536]{0:T(1024)S(1)} fusion(s32[128]{0:T(128)S(1)} %compare_select_fusion, f32[128]{0:T(128)S(1)} %fusion.55, f32[]{:T(128)} %constant.82.clone.1), kind=kCustom, calls=%fused_computation.62 | custom fusion | flops 128 | bytes 262148 | tf_op jit(solution)/shard_map/vmap()/scatter-add | solution.py:83
  17.6 0.3 divide_add_fusion.2
  18.1 0.3 divide_add_fusion.1
  18.6 0.3 divide_add_fusion
  19.1 1.0 %bitcast_multiply_fusion = f32[1,16,32,128]{3,2,1,0:T(8,128)} fusion(f32[1,1,16,32,128]{4,3,2,1,0:T(8,128)S(1)} %divide_add_fusion.3, f32[1,1,16,32,128]{4,3,2,1,0:T(8,128)S(1)} %divide_add_fusion, f32[1,1,16,32,128]{4,3,2,1,0:T(8,128)S(1)} %get-tuple-element.12, f32[1,1,16,32,128]{4,3,2,1,0:T(8,128)S(1)} %bitcast.67, f32[1,1,16,32,127]{4,3,2,1,0:T(8,128)S(1)} %fusion, ...), kind=kLoop, calls=%fused_computation.32 | loop fusion | flops 917504 | bytes 2332672 | tf_op jit(solution)/shard_map/vmap()/mul | solution.py:87
  20.1 0.3 convert_add_fusion
  20.5 0.7 cholesky.17
  21.4 0.6 compare_reduce_fusion
  22.1 17.7 %all-gather.2.cloned.1.call-done = f32[4,1,65536]{2,1,0:T(1,128)} async-done(((f32[1,1,65536]{2,1,0:T(1,128)}), f32[4,1,65536]{2,1,0:T(1,128)}) %all-gather.2.cloned.1.call-update) | async-done | bytes 1048592 | tf_op jit(solution)/shard_map/all_gather | solution.py:152
  39.7 2.2 %reduce_sum.16 = f32[65536]{0:T(1024)S(1)} reduce(f32[4,1,65536]{2,1,0:T(1,128)} %all-gather.2.cloned.1.call-done, f32[]{:T(128)} %constant.82.clone.1), dimensions={0,1}, to_apply=%region_4.5 | reduce | flops 196608 | bytes 1310724 | tf_op jit(solution)/shard_map/reduce_sum | solution.py:153
  41.9 0.7 dynamic-slice_subtract_fusion
  42.7 5.6 %all-to-all-start = ((f32[1,8,2048]{2,0,1:T(1,128)}), f32[1,8,2048]{2,0,1:T(1,128)S(1)}, u32[]{:S(2)}, u32[]{:S(2)}) async-start(f32[1,8,2048]{2,0,1:T(1,128)} %bitcast.15), calls=%async_computation | async-start | bytes 131072 | tf_op jit(solution)/shard_map/all_to_all | solution.py:159
  48.3 0.6 select_select_fusion
  49.0 0.6 custom-call.10
  49.7 5.5 %all-to-all-done = f32[1,8,2048]{2,0,1:T(1,128)S(1)} async-done(((f32[1,8,2048]{2,0,1:T(1,128)}), f32[1,8,2048]{2,0,1:T(1,128)S(1)}, u32[]{:S(2)}, u32[]{:S(2)}) %all-to-all-start) | async-done | bytes 65568 | tf_op jit(solution)/shard_map/all_to_all | solution.py:159
  55.2 0.3 fusion.27
  55.7 0.7 copy.33
  56.4 3.4 %all-to-all-start.1 = ((f32[8,1,2048]{2,1,0:T(1,128)}), f32[8,1,2048]{2,1,0:T(1,128)S(1)}, u32[]{:S(2)}, u32[]{:S(2)}) async-start(f32[8,1,2048]{2,1,0:T(1,128)} %copy.33), calls=%async_computation.1 | async-start | bytes 131072 | tf_op jit(solution)/shard_map/all_to_all | solution.py:161
  59.7 0.7 fusion.61
  60.4 6.2 %all-to-all-done.1 = f32[8,1,2048]{2,1,0:T(1,128)S(1)} async-done(((f32[8,1,2048]{2,1,0:T(1,128)}), f32[8,1,2048]{2,1,0:T(1,128)S(1)}, u32[]{:S(2)}, u32[]{:S(2)}) %all-to-all-start.1) | async-done | bytes 65568 | tf_op jit(solution)/shard_map/all_to_all | solution.py:161
  66.6 5.8 %all_gather.7 = f32[1,65536]{1,0:T(1,128)S(1)} all-gather(f32[1,16384]{1,0:T(1,128)S(1)} %bitcast.76), channel_id=1, replica_groups=mesh['src'=4,'ep'=8] {'src'}, dimensions={1}, use_global_device_ids=true | all-gather | bytes 327680 | tf_op jit(solution)/shard_map/all_gather | solution.py:162
  72.3 0.7 copy.42
  (55 shorter events, 2.9 us)
Async XLA Ops:
  7.2 1.1 %copy-start.1 = (f32[1,1,16,32,128]{4,3,2,1,0:T(8,128)S(1)}, f32[1,1,16,32,128]{4,3,2,1,0:T(8,128)}, u32[]{:S(2)}) copy-start(f32[1,1,16,32,128]{4,3,2,1,0:T(8,128)} %param.11) | copy-start | bytes 786436
  7.2 32.6 %all-gather.2.cloned.1.call-start = ((), (), s32[]{:S(2)}) async-start(), calls=%async_computation.2 | async-start | bytes 1310720 | tf_op jit(solution)/shard_map/all_gather | solution.py:152
  8.6 1.0 %copy-start.2 = (f32[1,1,16,32,128]{4,3,2,1,0:T(8,128)S(1)}, f32[1,1,16,32,128]{4,3,2,1,0:T(8,128)}, u32[]{:S(2)}) copy-start(f32[1,1,16,32,128]{4,3,2,1,0:T(8,128)} %param.10) | copy-start | bytes 786436
  9.7 0.7 copy-start.5
  10.4 1.2 %copy-start = (f32[1,16,32,128]{3,2,1,0:T(8,128)S(1)}, f32[1,16,32,128]{3,2,1,0:T(8,128)}, u32[]{:S(2)}) copy-start(f32[1,16,32,128]{3,2,1,0:T(8,128)} %param.9) | copy-start | bytes 786436
  14.2 0.7 copy-start.6
  15.1 1.2 %copy-start.7 = (f32[1,1,128]{2,1,0:T(1,128)S(1)}, f32[1,1,128]{2,1,0:T(1,128)}, u32[]{:S(2)}) copy-start(f32[1,1,128]{2,1,0:T(1,128)} %param.14) | copy-start | bytes 1540
  42.7 7.0 %copy-start.3 = (f32[6,2048]{1,0:T(8,128)S(1)}, f32[6,2048]{1,0:T(8,128)}, u32[]{:S(2)}) copy-start(f32[6,2048]{1,0:T(8,128)} %param.16) | copy-start | bytes 147460
  42.7 7.0 %copy-start.4 = (f32[6,2048]{1,0:T(8,128)S(1)}, f32[6,2048]{1,0:T(8,128)}, u32[]{:S(2)}) copy-start(f32[6,2048]{1,0:T(8,128)} %param.15) | copy-start | bytes 147460
  42.7 12.6 %all-to-all-start = ((f32[1,8,2048]{2,0,1:T(1,128)}), f32[1,8,2048]{2,0,1:T(1,128)S(1)}, u32[]{:S(2)}, u32[]{:S(2)}) async-start(f32[1,8,2048]{2,0,1:T(1,128)} %bitcast.15), calls=%async_computation | async-start | bytes 131072 | tf_op jit(solution)/shard_map/all_to_all | solution.py:159
  56.4 10.2 %all-to-all-start.1 = ((f32[8,1,2048]{2,1,0:T(1,128)}), f32[8,1,2048]{2,1,0:T(1,128)S(1)}, u32[]{:S(2)}, u32[]{:S(2)}) async-start(f32[8,1,2048]{2,1,0:T(1,128)} %copy.33), calls=%async_computation.1 | async-start | bytes 131072 | tf_op jit(solution)/shard_map/all_to_all | solution.py:161
Sparse Core Ops, SparseCore 0:
  20.2 19.4 all-gather.1
